TPU v7x, 32 devices: a whole 2x2x4 slice. The times are simulated.
32 devices in a mesh: band: 2 (over y), domain: 16 (over z, x, core).
Axes of the slice: x: 2, y: 2, z: 4, core: 2. Of those that a mesh axis runs over, the one named last changes fastest.
Arguments:
- orbitals: bfloat16 [128, 16, 32, 256], P('domain', None, None, 'band'), may hold values from -12 to 12
- potential: float32 [128, 16, 32], P('domain'), may hold values from -2 to 0
Outputs:
- filtered: bfloat16 [128, 16, 32, 256], P('domain', None, None, 'band')
- correlation: float32 [256, 256], P('band')
- projected: float32 [256, 256], P('band')
All inputs are finite; a program needn't handle non-finite values.
Results may differ from a plain program's by a relative error of at most 0.005.
Values may be sent and summed in bfloat16 or wider, within the bound.
No kernel may reach another device: no remote copies, remote signals or barrier semaphores. Data moves between devices by JAX's collectives and lax.ppermute only.
A program may use at most 64 MiB of HBM per device.

v0:
```python
import jax
import jax.numpy as jnp
from jax import lax
from jax.sharding import PartitionSpec as P

RADIUS = 4
stencil_weights = (-205.0 / 72.0, 8.0 / 5.0, -1.0 / 5.0, 8.0 / 315.0, -1.0 / 560.0)
spectrum_centre = 6.0
first_factor = -0.125
second_factor = -1.0 / 7.0
memory_factor = -1.0 / 7.0


def padded(block, sides, width):
    for axis, dim in sides:
        count = lax.axis_size(axis)
        forward = [(i, i + 1) for i in range(count - 1)]
        forward.append((count - 1, 0))
        backward = [(target, source) for source, target in forward]
        low = lax.ppermute(
            lax.slice_in_dim(block, block.shape[dim] - width, None, axis=dim), axis, forward
        )
        high = lax.ppermute(lax.slice_in_dim(block, 0, width, axis=dim), axis, backward)
        block = jnp.concatenate([low, block, high], axis=dim)
    return block


def planes_of(extended, first_plane, planes):
    return lax.slice_in_dim(extended, first_plane, first_plane + planes, axis=0)


def hamiltonian(extended, potential, planes):
    middle = planes_of(extended, RADIUS, planes)
    summed = 3.0 * stencil_weights[0] * middle
    for offset in range(1, RADIUS + 1):
        beside = planes_of(extended, RADIUS + offset, planes) + planes_of(
            extended, RADIUS - offset, planes
        )
        beside = beside + jnp.roll(middle, offset, axis=1) + jnp.roll(middle, -offset, axis=1)
        beside = beside + jnp.roll(middle, offset, axis=2) + jnp.roll(middle, -offset, axis=2)
        summed = summed + stencil_weights[offset] * beside
    return -0.5 * summed + potential[:, :, :, None] * middle


def widened(values):
    return padded(values, (("domain", 0),), RADIUS)


def energy_block(filtered, potential, cell_count):
    extended = padded(filtered, (("domain", 0),), RADIUS).astype(jnp.float32)
    applied = hamiltonian(extended, potential, filtered.shape[0]).astype(jnp.bfloat16)
    return applied.reshape(cell_count, filtered.shape[3])


def shards(orbitals, potential):
    planes = orbitals.shape[0]
    initial = orbitals.astype(jnp.float32)
    extended = widened(orbitals).astype(jnp.float32)
    first = (
        (hamiltonian(extended, potential, planes) - spectrum_centre * initial) * first_factor
    ).astype(jnp.bfloat16)
    first_wide = widened(first).astype(jnp.float32)
    first_own = planes_of(first_wide, RADIUS, planes)
    filtered = (
        (hamiltonian(first_wide, potential, planes) - spectrum_centre * first_own) * second_factor
        + memory_factor * initial
    ).astype(jnp.bfloat16)
    cell_count = planes * filtered.shape[1] * filtered.shape[2]
    cell_weight = 1.0 / (cell_count * lax.axis_size("domain"))
    own_block = filtered.reshape(cell_count, filtered.shape[3])
    applied = energy_block(filtered, potential, cell_count)
    piece = lax.all_gather(own_block, "band", axis=1, tiled=True)
    correlation_piece = jnp.einsum(
        "cb,ck->bk", own_block, piece, preferred_element_type=jnp.float32
    )
    energy_piece = jnp.einsum("cb,ck->bk", applied, piece, preferred_element_type=jnp.float32)
    partial_terms = jnp.stack((correlation_piece, energy_piece))
    summed = lax.psum(partial_terms, "domain") * cell_weight
    correlation = summed[0]
    projected = summed[1]
    return (filtered, correlation, projected)


def solution(mesh):
    placed = (P("domain", None, None, "band"), P("domain", None, None))
    return jax.shard_map(
        shards,
        mesh=mesh,
        in_specs=placed,
        out_specs=(P("domain", None, None, "band"), P("band", None), P("band", None)),
        check_vma=False,
    )
```

profile of v0, /device:TPU:1, one launch (start us, length us, event | category | flops | bytes accessed | tf_op | source)
XLA Modules:
  0.0 240.1 jit_solution(3765272262205652214)
XLA Ops:
  7.2 1.3 fusion.132
  8.7 2.6 %collective-permute-start = (bf16[4,16,32,128]{3,2,1,0:T(8,128)(2,1)S(1)}, bf16[4,16,32,128]{3,2,1,0:T(8,128)(2,1)S(1)}, u32[]{:S(2)}, u32[]{:S(2)}) collective-permute-start(bf16[4,16,32,128]{3,2,1,0:T(8,128)(2,1)S(1)} %get-tuple-element.103), channel_id=1, source_target_pairs={{0,1},{1,2},{2,3},{3,4},{4,5},{5,6},{6,7},{7,8},{8,9},{9,10},{10,1... | collective-permute-start | bytes 1572872 | tf_op jit(solution)/shard_map/ppermute | solution.py:20
  11.3 6.8 %collective-permute-done.1 = bf16[4,16,32,128]{3,2,1,0:T(8,128)(2,1)S(1)} collective-permute-done((bf16[4,16,32,128]{3,2,1,0:T(8,128)(2,1)S(1)}, bf16[4,16,32,128]{3,2,1,0:T(8,128)(2,1)S(1)}, u32[]{:S(2)}, u32[]{:S(2)}) %collective-permute-start.1) | collective-permute-done | bytes 524320 | tf_op jit(solution)/shard_map/ppermute | solution.py:23
  18.1 4.9 %collective-permute-done = bf16[4,16,32,128]{3,2,1,0:T(8,128)(2,1)S(1)} collective-permute-done((bf16[4,16,32,128]{3,2,1,0:T(8,128)(2,1)S(1)}, bf16[4,16,32,128]{3,2,1,0:T(8,128)(2,1)S(1)}, u32[]{:S(2)}, u32[]{:S(2)}) %collective-permute-start) | collective-permute-done | bytes 524320 | tf_op jit(solution)/shard_map/ppermute | solution.py:20
  23.4 2.5 %fusion.128 = (f32[8,15,32,128]{3,2,1,0:T(8,128)}, f32[8,15,32,128]{3,2,1,0:T(8,128)}) fusion(f32[16,16,32,128]{3,2,1,0:T(8,128)S(1)} %maximum_convert_fusion), kind=kLoop, calls=%fused_computation.157 | loop fusion | bytes 7864320 | tf_op jit(solution)/shard_map/jit(_roll_static)/slice | solution.py:39
  25.8 0.7 fusion.129
  27.2 2.4 fusion.125
  29.6 0.8 fusion.126
  31.1 0.8 fusion.124
  31.9 2.2 fusion.121
  34.1 0.8 fusion.122
  35.5 0.9 fusion.120
  36.5 2.1 fusion.117
  38.6 0.9 fusion.118
  40.0 0.9 fusion.116
  41.6 10.1 %fusion.2 = bf16[8,16,32,128]{3,2,1,0:T(8,128)(2,1)S(1)} fusion(bf16[8,16,32,128]{3,2,1,0:T(8,128)(2,1)S(1)} %copy-done.2, f32[16,16,32,128]{3,2,1,0:T(8,128)S(1)} %maximum_convert_fusion, f32[8,15,32,128]{3,2,1,0:T(8,128)} %get-tuple-element.90, f32[8,1,32,128]{3,2,1,0:T(8,128)} %get-tuple-element.92, f32[8,1,32,128]{3,2,1,0:T(8,128)} %get-tuple-element.91, ...), kind=kLoop, calls=%fused_computation.4 | loop fusion | flops 27787264 | bytes 54542336 | tf_op jit(solution)/shard_map/convert_element_type | solution.py:61
  51.7 2.4 %collective-permute-start.3 = (bf16[4,16,32,128]{3,2,1,0:T(8,128)(2,1)S(1)}, bf16[4,16,32,128]{3,2,1,0:T(8,128)(2,1)S(1)}, u32[]{:S(2)}, u32[]{:S(2)}) collective-permute-start(bf16[4,16,32,128]{3,2,1,0:T(8,128)(2,1)S(1)} %get-tuple-element.102), channel_id=1, source_target_pairs={{1,0},{2,1},{3,2},{4,3},{5,4},{6,5},{7,6},{8,7},{9,8},{10,9},{11,1... | collective-permute-start | bytes 1572872 | tf_op jit(solution)/shard_map/ppermute | solution.py:23
  54.5 12.2 %collective-permute-done.3 = bf16[4,16,32,128]{3,2,1,0:T(8,128)(2,1)S(1)} collective-permute-done((bf16[4,16,32,128]{3,2,1,0:T(8,128)(2,1)S(1)}, bf16[4,16,32,128]{3,2,1,0:T(8,128)(2,1)S(1)}, u32[]{:S(2)}, u32[]{:S(2)}) %collective-permute-start.3) | collective-permute-done | bytes 524320 | tf_op jit(solution)/shard_map/ppermute | solution.py:23
  67.1 2.5 %fusion.113 = (f32[8,15,32,128]{3,2,1,0:T(8,128)}, f32[8,15,32,128]{3,2,1,0:T(8,128)}) fusion(f32[16,16,32,128]{3,2,1,0:T(8,128)S(1)} %maximum_convert_fusion.1), kind=kLoop, calls=%fused_computation.142 | loop fusion | bytes 7864320 | tf_op jit(solution)/shard_map/jit(_roll_static)/slice | solution.py:39
  70.8 2.4 fusion.110
  73.2 0.8 fusion.111
  74.7 0.8 fusion.109
  75.5 2.3 fusion.106
  78.5 0.9 fusion.105
  79.4 2.1 fusion.102
  81.5 1.8 fusion.100
  83.3 0.9 fusion.101
  85.0 10.1 %fusion.4 = bf16[8,16,32,128]{3,2,1,0:T(8,128)(2,1)S(1)} fusion(bf16[8,16,32,128]{3,2,1,0:T(8,128)(2,1)S(1)} %copy-done.2, f32[16,16,32,128]{3,2,1,0:T(8,128)S(1)} %maximum_convert_fusion.1, f32[8,15,32,128]{3,2,1,0:T(8,128)} %get-tuple-element.60, f32[8,1,32,128]{3,2,1,0:T(8,128)} %get-tuple-element.62, f32[8,1,32,128]{3,2,1,0:T(8,128)S(1)} %get-tuple-element.61, ...), kind=kLoop, calls=%fused_computation.6 | loop fusion | flops 28311552 | bytes 54542336 | tf_op jit(solution)/shard_map/convert_element_type | solution.py:67
  95.3 1.7 collective-permute-start.4
  97.3 12.6 %collective-permute-done.5 = bf16[4,16,32,128]{3,2,1,0:T(8,128)(2,1)S(1)} collective-permute-done((bf16[4,16,32,128]{3,2,1,0:T(8,128)(2,1)S(1)}, bf16[4,16,32,128]{3,2,1,0:T(8,128)(2,1)S(1)}, u32[]{:S(2)}, u32[]{:S(2)}) %collective-permute-start.5) | collective-permute-done | bytes 524320 | tf_op jit(solution)/shard_map/ppermute | solution.py:23
  109.9 1.6 maximum_convert_fusion.2
  111.5 2.5 %fusion.98 = (f32[8,15,32,128]{3,2,1,0:T(8,128)}, f32[8,15,32,128]{3,2,1,0:T(8,128)}) fusion(f32[16,16,32,128]{3,2,1,0:T(8,128)S(1)} %maximum_convert_fusion.2), kind=kLoop, calls=%fused_computation.127 | loop fusion | bytes 7864320 | tf_op jit(solution)/shard_map/jit(_roll_static)/slice | solution.py:39
  115.3 2.4 fusion.95
  117.6 0.9 fusion.96
  119.1 0.8 fusion.94
  120.0 1.5 fusion.91
  121.5 0.8 fusion.92
  122.3 0.9 fusion.90
  123.2 2.1 fusion.87
  125.4 1.1 fusion.88
  126.5 0.9 fusion.86
  127.4 0.7 maximum_convert_fusion.3
  129.2 10.8 %fusion.13 = bf16[8,16,32,128]{3,2,1,0:T(8,128)(2,1)} fusion(f32[16,16,32,128]{3,2,1,0:T(8,128)S(1)} %maximum_convert_fusion.2, f32[8,15,32,128]{3,2,1,0:T(8,128)} %get-tuple-element.30, f32[8,1,32,128]{3,2,1,0:T(8,128)} %get-tuple-element.32, f32[8,1,32,128]{3,2,1,0:T(8,128)} %get-tuple-element.31, f32[8,15,32,128]{3,2,1,0:T(8,128)} %get-tuple-element.29, ...), kind=kLoop, calls=%fused_computation.16 | loop fusion | flops 25690112 | bytes 53493760 | tf_op jit(solution)/shard_map/convert_element_type | solution.py:51
  140.1 2.2 convolution_bitcast_fusion.1
  143.1 0.7 pad_maximum_fusion
  143.9 87.7 %all-reduce.2.cloned.1.call-done = f32[2,128,256]{2,1,0:T(8,128)} async-done(((f32[2,128,256]{2,1,0:T(8,128)}), f32[2,128,256]{2,1,0:T(8,128)}) %all-reduce.2.cloned.1.call-update) | async-done | bytes 262160 | tf_op jit(solution)/shard_map/psum | solution.py:78
  231.6 1.0 broadcast_multiply_fusion
  232.5 0.7 slice_bitcast_fusion
  (44 shorter events, 12.0 us)
Async XLA Ops:
  7.2 15.9 %copy-start.2 = (bf16[8,16,32,128]{3,2,1,0:T(8,128)(2,1)S(1)}, bf16[8,16,32,128]{3,2,1,0:T(8,128)(2,1)}, u32[]{:S(2)}) copy-start(bf16[8,16,32,128]{3,2,1,0:T(8,128)(2,1)} %param.2) | copy-start | bytes 3145732
  7.2 132.9 %all-gather.2.cloned.1.call-start = ((), (), s32[]{:S(2)}) async-start(), calls=%async_computation | async-start | bytes 3145728 | tf_op jit(solution)/shard_map/all_gather | solution.py:72
  8.6 9.5 %collective-permute-start.1 = (bf16[4,16,32,128]{3,2,1,0:T(8,128)(2,1)S(1)}, bf16[4,16,32,128]{3,2,1,0:T(8,128)(2,1)S(1)}, u32[]{:S(2)}, u32[]{:S(2)}) collective-permute-start(bf16[4,16,32,128]{3,2,1,0:T(8,128)(2,1)S(1)} %get-tuple-element.104), channel_id=1, source_target_pairs={{1,0},{2,1},{3,2},{4,3},{5,4},{6,5},{7,6},{8,7},{9,8},{10,9},{11,1... | collective-permute-start | bytes 1572872 | tf_op jit(solution)/shard_map/ppermute | solution.py:23
  8.7 14.4 %collective-permute-start = (bf16[4,16,32,128]{3,2,1,0:T(8,128)(2,1)S(1)}, bf16[4,16,32,128]{3,2,1,0:T(8,128)(2,1)S(1)}, u32[]{:S(2)}, u32[]{:S(2)}) collective-permute-start(bf16[4,16,32,128]{3,2,1,0:T(8,128)(2,1)S(1)} %get-tuple-element.103), channel_id=1, source_target_pairs={{0,1},{1,2},{2,3},{3,4},{4,5},{5,6},{6,7},{7,8},{8,9},{9,10},{10,1... | collective-permute-start | bytes 1572872 | tf_op jit(solution)/shard_map/ppermute | solution.py:20
  40.0 1.6 copy-start.5
  51.7 15.0 %collective-permute-start.3 = (bf16[4,16,32,128]{3,2,1,0:T(8,128)(2,1)S(1)}, bf16[4,16,32,128]{3,2,1,0:T(8,128)(2,1)S(1)}, u32[]{:S(2)}, u32[]{:S(2)}) collective-permute-start(bf16[4,16,32,128]{3,2,1,0:T(8,128)(2,1)S(1)} %get-tuple-element.102), channel_id=1, source_target_pairs={{1,0},{2,1},{3,2},{4,3},{5,4},{6,5},{7,6},{8,7},{9,8},{10,9},{11,1... | collective-permute-start | bytes 1572872 | tf_op jit(solution)/shard_map/ppermute | solution.py:23
  54.2 12.6 %collective-permute-start.2 = (bf16[4,16,32,128]{3,2,1,0:T(8,128)(2,1)S(1)}, bf16[4,16,32,128]{3,2,1,0:T(8,128)(2,1)S(1)}, u32[]{:S(2)}, u32[]{:S(2)}) collective-permute-start(bf16[4,16,32,128]{3,2,1,0:T(8,128)(2,1)S(1)} %get-tuple-element.101), channel_id=1, source_target_pairs={{0,1},{1,2},{2,3},{3,4},{4,5},{5,6},{6,7},{7,8},{8,9},{9,10},{10,1... | collective-permute-start | bytes 1572872 | tf_op jit(solution)/shard_map/ppermute | solution.py:20
  95.1 1.9 copy-start
  95.2 14.7 %collective-permute-start.5 = (bf16[4,16,32,128]{3,2,1,0:T(8,128)(2,1)S(1)}, bf16[4,16,32,128]{3,2,1,0:T(8,128)(2,1)S(1)}, u32[]{:S(2)}, u32[]{:S(2)}) collective-permute-start(bf16[4,16,32,128]{3,2,1,0:T(8,128)(2,1)S(1)} %get-tuple-element.100), channel_id=1, source_target_pairs={{1,0},{2,1},{3,2},{4,3},{5,4},{6,5},{7,6},{8,7},{9,8},{10,9},{11,1... | collective-permute-start | bytes 1572872 | tf_op jit(solution)/shard_map/ppermute | solution.py:23
  95.3 14.6 %collective-permute-start.4 = (bf16[4,16,32,128]{3,2,1,0:T(8,128)(2,1)S(1)}, bf16[4,16,32,128]{3,2,1,0:T(8,128)(2,1)S(1)}, u32[]{:S(2)}, u32[]{:S(2)}) collective-permute-start(bf16[4,16,32,128]{3,2,1,0:T(8,128)(2,1)S(1)} %get-tuple-element.99), channel_id=1, source_target_pairs={{0,1},{1,2},{2,3},{3,4},{4,5},{5,6},{6,7},{7,8},{8,9},{9,10},{10,1... | collective-permute-start | bytes 1572872 | tf_op jit(solution)/shard_map/ppermute | solution.py:20
  97.0 134.5 %all-reduce.2.cloned.1.call-start = ((), (), s32[]{:S(2)}) async-start(), calls=%async_computation.1 | async-start | bytes 524288 | tf_op jit(solution)/shard_map/psum | solution.py:78
  125.4 2.0 copy-start.1
  140.1 2.3 copy-start.4
  140.1 2.5 %copy-start.3 = (bf16[4096,256]{1,0:T(8,128)(2,1)S(1)}, bf16[4096,256]{1,0:T(8,128)(2,1)}, u32[]{:S(2)}) copy-start(bf16[4096,256]{1,0:T(8,128)(2,1)} %all-gather.2.cloned.1.call-done) | copy-start | bytes 6291460
Sparse Core Ops, SparseCore 0:
  97.2 33.2 all-gather.1
  144.0 87.4 all-reduce.1
where the time goes:
time: 240 us
  waiting for transfers between devices  124 us (52%)
  local copies, waits for them, and re-layouts  54.1 us (23%)
  other arithmetic  37 us (15%)
  between operations  14.3 us (6%)
  starting transfers between devices  7.59 us (3%)
  matrix products  2.76 us (1%)
    psum x1, waiting for transfers between devices, shards(): summed = lax.psum(partial_terms, 'domain') * cell_weight  87.7 us
    slice x24, local copies, waits for them, and re-layouts, hamiltonian(): jnp.roll(middle, -offset, axis=1)  35.2 us
    ppermute x3, waiting for transfers between devices, padded(): lax.ppermute(lax.slice_in_dim(block, 0, width, axis=dim), axis, backward)  31.6 us
    slice x21, local copies, waits for them, and re-layouts, hamiltonian(): jnp.roll(middle, -offset, axis=2)  16.5 us
    convert_element_type x1, other arithmetic, energy_block(): hamiltonian(extended, potential, filtered.shape[0]).astype(jnp.bfloat16)  10.8 us
    convert_element_type x1, other arithmetic, shards(): filtered = ((hamiltonian(first_wide, potential, planes) - spectrum_centre...  10.1 us
    convert_element_type x1, other arithmetic, shards(): first = ((hamiltonian(extended, potential, planes) - spectrum_centre * in...  10.1 us
    ppermute x3, waiting for transfers between devices, padded(): lax.ppermute(lax.slice_in_dim(block, block.shape[dim] - width, None, axis...  4.95 us
  transfers between devices with their start and end apart: 8, of which 5 were waited for; matrix products, arithmetic and copies ran while one was open for 13% of the time, Pallas kernels for 0%

commit v1 on v0

--- a/solution.py
+++ b/solution.py
@@ -53,6 +53,10 @@
 
 
 def shards(orbitals, potential):
+
+    def place_sides(message):
+        return jnp.sum(lax.all_gather(message, "domain"), axis=0)
+
     planes = orbitals.shape[0]
     initial = orbitals.astype(jnp.float32)
     extended = widened(orbitals).astype(jnp.float32)
@@ -75,7 +79,7 @@
     )
     energy_piece = jnp.einsum("cb,ck->bk", applied, piece, preferred_element_type=jnp.float32)
     partial_terms = jnp.stack((correlation_piece, energy_piece))
-    summed = lax.psum(partial_terms, "domain") * cell_weight
+    summed = place_sides(partial_terms) * cell_weight
     correlation = summed[0]
     projected = summed[1]
     return (filtered, correlation, projected)

time: 240 us -> 204 us (0.85)
  waiting for transfers between devices: 124 us -> 85.8 us
    psum x1 -> x0, waiting for transfers between devices: 87.7 us -> none  [shards(): summed = lax.psum(partial_terms, 'domain') * cell_weight]
    all_gather x0 -> x1, waiting for transfers between devices: none -> 49.1 us  [place_sides(): return jnp.sum(lax.all_gather(message, 'domain'), axis=0)]
    reduce_sum x0 -> x1, other arithmetic: none -> 2.48 us  [place_sides(): return jnp.sum(lax.all_gather(message, 'domain'), axis=0)]
  transfers between devices with their start and end apart: 8 -> 8, of which waited for: 5 -> 5; matrix products, arithmetic and copies ran while one was open for 13% -> 15% of each run, Pallas kernels for 0% -> 0%
where the time goes in v1:
time: 204 us; the launch traced here: 203 us
  waiting for transfers between devices  85.8 us (42%)
  local copies, waits for them, and re-layouts  54.1 us (27%)
  other arithmetic  38.5 us (19%)
  between operations  14.3 us (7%)
  starting transfers between devices  7.59 us (4%)
  matrix products  2.76 us (1%)
    all_gather x1, waiting for transfers between devices, place_sides(): return jnp.sum(lax.all_gather(message, 'domain'), axis=0)  49.1 us
    slice x24, local copies, waits for them, and re-layouts, hamiltonian(): jnp.roll(middle, -offset, axis=1)  35.2 us
    ppermute x3, waiting for transfers between devices, padded(): lax.ppermute(lax.slice_in_dim(block, 0, width, axis=dim), axis, backward)  31.6 us
    slice x21, local copies, waits for them, and re-layouts, hamiltonian(): jnp.roll(middle, -offset, axis=2)  16.5 us
    convert_element_type x1, other arithmetic, energy_block(): hamiltonian(extended, potential, filtered.shape[0]).astype(jnp.bfloat16)  10.8 us
    convert_element_type x1, other arithmetic, shards(): filtered = ((hamiltonian(first_wide, potential, planes) - spectrum_centre...  10.1 us
    convert_element_type x1, other arithmetic, shards(): first = ((hamiltonian(extended, potential, planes) - spectrum_centre * in...  10.1 us
    ppermute x3, waiting for transfers between devices, padded(): lax.ppermute(lax.slice_in_dim(block, block.shape[dim] - width, None, axis...  4.95 us
  transfers between devices with their start and end apart: 8, of which 5 were waited for; matrix products, arithmetic and copies ran while one was open for 15% of the time, Pallas kernels for 0%

profile of v1, /device:TPU:1, one launch (start us, length us, event | category | flops | bytes accessed | tf_op | source)
XLA Modules:
  0.0 203.1 jit_solution(14241122247578907194)
XLA Ops:
  7.2 1.3 fusion.132
  8.7 2.6 %collective-permute-start = (bf16[4,16,32,128]{3,2,1,0:T(8,128)(2,1)S(1)}, bf16[4,16,32,128]{3,2,1,0:T(8,128)(2,1)S(1)}, u32[]{:S(2)}, u32[]{:S(2)}) collective-permute-start(bf16[4,16,32,128]{3,2,1,0:T(8,128)(2,1)S(1)} %get-tuple-element.103), channel_id=1, source_target_pairs={{0,1},{1,2},{2,3},{3,4},{4,5},{5,6},{6,7},{7,8},{8,9},{9,10},{10,1... | collective-permute-start | bytes 1572872 | tf_op jit(solution)/shard_map/ppermute | solution.py:20
  11.3 6.8 %collective-permute-done.1 = bf16[4,16,32,128]{3,2,1,0:T(8,128)(2,1)S(1)} collective-permute-done((bf16[4,16,32,128]{3,2,1,0:T(8,128)(2,1)S(1)}, bf16[4,16,32,128]{3,2,1,0:T(8,128)(2,1)S(1)}, u32[]{:S(2)}, u32[]{:S(2)}) %collective-permute-start.1) | collective-permute-done | bytes 524320 | tf_op jit(solution)/shard_map/ppermute | solution.py:23
  18.1 4.9 %collective-permute-done = bf16[4,16,32,128]{3,2,1,0:T(8,128)(2,1)S(1)} collective-permute-done((bf16[4,16,32,128]{3,2,1,0:T(8,128)(2,1)S(1)}, bf16[4,16,32,128]{3,2,1,0:T(8,128)(2,1)S(1)}, u32[]{:S(2)}, u32[]{:S(2)}) %collective-permute-start) | collective-permute-done | bytes 524320 | tf_op jit(solution)/shard_map/ppermute | solution.py:20
  23.4 2.5 %fusion.128 = (f32[8,15,32,128]{3,2,1,0:T(8,128)}, f32[8,15,32,128]{3,2,1,0:T(8,128)}) fusion(f32[16,16,32,128]{3,2,1,0:T(8,128)S(1)} %maximum_convert_fusion), kind=kLoop, calls=%fused_computation.157 | loop fusion | bytes 7864320 | tf_op jit(solution)/shard_map/jit(_roll_static)/slice | solution.py:39
  25.8 0.7 fusion.129
  27.2 2.4 %fusion.125 = (f32[8,14,32,128]{3,2,1,0:T(8,128)}, f32[8,14,32,128]{3,2,1,0:T(8,128)}) fusion(f32[16,16,32,128]{3,2,1,0:T(8,128)S(1)} %maximum_convert_fusion), kind=kLoop, calls=%fused_computation.154 | loop fusion | bytes 7340032 | tf_op jit(solution)/shard_map/jit(_roll_static)/slice | solution.py:39
  29.6 0.8 fusion.126
  31.1 0.8 fusion.124
  31.9 2.2 %fusion.121 = (f32[8,13,32,128]{3,2,1,0:T(8,128)}, f32[8,13,32,128]{3,2,1,0:T(8,128)}) fusion(f32[16,16,32,128]{3,2,1,0:T(8,128)S(1)} %maximum_convert_fusion), kind=kLoop, calls=%fused_computation.150 | loop fusion | bytes 6815744 | tf_op jit(solution)/shard_map/jit(_roll_static)/slice | solution.py:39
  34.1 0.8 fusion.122
  35.5 0.9 fusion.120
  36.5 2.1 %fusion.117 = (f32[8,12,32,128]{3,2,1,0:T(8,128)}, f32[8,12,32,128]{3,2,1,0:T(8,128)}) fusion(f32[16,16,32,128]{3,2,1,0:T(8,128)S(1)} %maximum_convert_fusion), kind=kLoop, calls=%fused_computation.146 | loop fusion | bytes 6291456 | tf_op jit(solution)/shard_map/jit(_roll_static)/slice | solution.py:39
  38.6 0.9 fusion.118
  40.0 0.9 fusion.116
  41.6 10.1 %fusion.2 = bf16[8,16,32,128]{3,2,1,0:T(8,128)(2,1)S(1)} fusion(bf16[8,16,32,128]{3,2,1,0:T(8,128)(2,1)S(1)} %copy-done.2, f32[16,16,32,128]{3,2,1,0:T(8,128)S(1)} %maximum_convert_fusion, f32[8,15,32,128]{3,2,1,0:T(8,128)} %get-tuple-element.90, f32[8,1,32,128]{3,2,1,0:T(8,128)} %get-tuple-element.92, f32[8,1,32,128]{3,2,1,0:T(8,128)} %get-tuple-element.91, ...), kind=kLoop, calls=%fused_computation.4 | loop fusion | flops 27787264 | bytes 54542336 | tf_op jit(solution)/shard_map/convert_element_type | solution.py:65
  51.7 2.4 %collective-permute-start.3 = (bf16[4,16,32,128]{3,2,1,0:T(8,128)(2,1)S(1)}, bf16[4,16,32,128]{3,2,1,0:T(8,128)(2,1)S(1)}, u32[]{:S(2)}, u32[]{:S(2)}) collective-permute-start(bf16[4,16,32,128]{3,2,1,0:T(8,128)(2,1)S(1)} %get-tuple-element.102), channel_id=1, source_target_pairs={{1,0},{2,1},{3,2},{4,3},{5,4},{6,5},{7,6},{8,7},{9,8},{10,9},{11,1... | collective-permute-start | bytes 1572872 | tf_op jit(solution)/shard_map/ppermute | solution.py:23
  54.5 12.2 %collective-permute-done.3 = bf16[4,16,32,128]{3,2,1,0:T(8,128)(2,1)S(1)} collective-permute-done((bf16[4,16,32,128]{3,2,1,0:T(8,128)(2,1)S(1)}, bf16[4,16,32,128]{3,2,1,0:T(8,128)(2,1)S(1)}, u32[]{:S(2)}, u32[]{:S(2)}) %collective-permute-start.3) | collective-permute-done | bytes 524320 | tf_op jit(solution)/shard_map/ppermute | solution.py:23
  67.1 2.5 %fusion.113 = (f32[8,15,32,128]{3,2,1,0:T(8,128)}, f32[8,15,32,128]{3,2,1,0:T(8,128)}) fusion(f32[16,16,32,128]{3,2,1,0:T(8,128)S(1)} %maximum_convert_fusion.1), kind=kLoop, calls=%fused_computation.142 | loop fusion | bytes 7864320 | tf_op jit(solution)/shard_map/jit(_roll_static)/slice | solution.py:39
  70.8 2.4 %fusion.110 = (f32[8,14,32,128]{3,2,1,0:T(8,128)}, f32[8,14,32,128]{3,2,1,0:T(8,128)}) fusion(f32[16,16,32,128]{3,2,1,0:T(8,128)S(1)} %maximum_convert_fusion.1), kind=kLoop, calls=%fused_computation.139 | loop fusion | bytes 7340032 | tf_op jit(solution)/shard_map/jit(_roll_static)/slice | solution.py:39
  73.2 0.8 fusion.111
  74.7 0.8 fusion.109
  75.5 2.3 %fusion.106 = (f32[8,13,32,128]{3,2,1,0:T(8,128)}, f32[8,13,32,128]{3,2,1,0:T(8,128)}) fusion(f32[16,16,32,128]{3,2,1,0:T(8,128)S(1)} %maximum_convert_fusion.1), kind=kLoop, calls=%fused_computation.135 | loop fusion | bytes 6815744 | tf_op jit(solution)/shard_map/jit(_roll_static)/slice | solution.py:39
  78.5 0.9 fusion.105
  79.4 2.1 %fusion.102 = (f32[8,12,32,128]{3,2,1,0:T(8,128)}, f32[8,12,32,128]{3,2,1,0:T(8,128)}) fusion(f32[16,16,32,128]{3,2,1,0:T(8,128)S(1)} %maximum_convert_fusion.1), kind=kLoop, calls=%fused_computation.131 | loop fusion | bytes 6291456 | tf_op jit(solution)/shard_map/jit(_roll_static)/slice | solution.py:39
  81.5 1.8 fusion.100
  83.3 0.9 fusion.101
  85.0 10.1 %fusion.4 = bf16[8,16,32,128]{3,2,1,0:T(8,128)(2,1)S(1)} fusion(bf16[8,16,32,128]{3,2,1,0:T(8,128)(2,1)S(1)} %copy-done.2, f32[16,16,32,128]{3,2,1,0:T(8,128)S(1)} %maximum_convert_fusion.1, f32[8,15,32,128]{3,2,1,0:T(8,128)} %get-tuple-element.60, f32[8,1,32,128]{3,2,1,0:T(8,128)} %get-tuple-element.62, f32[8,1,32,128]{3,2,1,0:T(8,128)S(1)} %get-tuple-element.61, ...), kind=kLoop, calls=%fused_computation.6 | loop fusion | flops 28311552 | bytes 54542336 | tf_op jit(solution)/shard_map/convert_element_type | solution.py:71
  95.3 1.7 collective-permute-start.4
  97.3 12.6 %collective-permute-done.5 = bf16[4,16,32,128]{3,2,1,0:T(8,128)(2,1)S(1)} collective-permute-done((bf16[4,16,32,128]{3,2,1,0:T(8,128)(2,1)S(1)}, bf16[4,16,32,128]{3,2,1,0:T(8,128)(2,1)S(1)}, u32[]{:S(2)}, u32[]{:S(2)}) %collective-permute-start.5) | collective-permute-done | bytes 524320 | tf_op jit(solution)/shard_map/ppermute | solution.py:23
  109.9 1.6 maximum_convert_fusion.2
  111.5 2.5 %fusion.98 = (f32[8,15,32,128]{3,2,1,0:T(8,128)}, f32[8,15,32,128]{3,2,1,0:T(8,128)}) fusion(f32[16,16,32,128]{3,2,1,0:T(8,128)S(1)} %maximum_convert_fusion.2), kind=kLoop, calls=%fused_computation.127 | loop fusion | bytes 7864320 | tf_op jit(solution)/shard_map/jit(_roll_static)/slice | solution.py:39
  113.9 0.7 fusion.99
  115.3 2.4 %fusion.95 = (f32[8,14,32,128]{3,2,1,0:T(8,128)}, f32[8,14,32,128]{3,2,1,0:T(8,128)}) fusion(f32[16,16,32,128]{3,2,1,0:T(8,128)S(1)} %maximum_convert_fusion.2), kind=kLoop, calls=%fused_computation.124 | loop fusion | bytes 7340032 | tf_op jit(solution)/shard_map/jit(_roll_static)/slice | solution.py:39
  117.6 0.9 fusion.96
  119.1 0.8 fusion.94
  120.0 1.5 fusion.91
  121.5 0.8 fusion.92
  122.3 0.9 fusion.90
  123.2 2.1 %fusion.87 = (f32[8,12,32,128]{3,2,1,0:T(8,128)}, f32[8,12,32,128]{3,2,1,0:T(8,128)}) fusion(f32[16,16,32,128]{3,2,1,0:T(8,128)S(1)} %maximum_convert_fusion.2), kind=kLoop, calls=%fused_computation.116 | loop fusion | bytes 6291456 | tf_op jit(solution)/shard_map/jit(_roll_static)/slice | solution.py:39
  125.4 1.1 fusion.88
  126.5 0.9 fusion.86
  127.4 0.7 maximum_convert_fusion.3
  129.2 10.8 %fusion.13 = bf16[8,16,32,128]{3,2,1,0:T(8,128)(2,1)} fusion(f32[16,16,32,128]{3,2,1,0:T(8,128)S(1)} %maximum_convert_fusion.2, f32[8,15,32,128]{3,2,1,0:T(8,128)} %get-tuple-element.30, f32[8,1,32,128]{3,2,1,0:T(8,128)} %get-tuple-element.32, f32[8,1,32,128]{3,2,1,0:T(8,128)} %get-tuple-element.31, f32[8,15,32,128]{3,2,1,0:T(8,128)} %get-tuple-element.29, ...), kind=kLoop, calls=%fused_computation.16 | loop fusion | flops 25690112 | bytes 53493760 | tf_op jit(solution)/shard_map/convert_element_type | solution.py:51
  140.1 2.2 %convolution_bitcast_fusion.1 = f32[1,128,256]{2,1,0:T(8,128)S(1)} fusion(bf16[4096,128]{1,0:T(8,128)(2,1)S(1)} %bitcast.16, bf16[4096,256]{1,0:T(8,128)(2,1)} %all-gather.4.cloned.1.call-done), kind=kOutput, calls=%fused_computation.103 | convolution fusion | flops 268435456 | bytes 3276800 | tf_op jit(solution)/shard_map/cb,ck->bk/dot_general | solution.py:77
  143.9 49.1 %all-gather.6.cloned.1.call-done = f32[32,128,256]{2,1,0:T(8,128)} async-done(((f32[2,128,256]{2,1,0:T(8,128)}), f32[32,128,256]{2,1,0:T(8,128)}) %all-gather.6.cloned.1.call-update) | async-done | bytes 4194320 | tf_op jit(solution)/shard_map/all_gather | solution.py:58
  193.0 2.5 %reduce_sum.9 = f32[2,128,256]{2,1,0:T(8,128)S(1)} reduce(f32[16,2,128,256]{3,2,1,0:T(8,128)} %bitcast.17, f32[]{:T(128)} %constant.9.clone.1), dimensions={0}, to_apply=%region_0.1 | reduce | flops 983040 | bytes 4456452 | tf_op jit(solution)/shard_map/reduce_sum | solution.py:58
  195.5 0.7 slice_bitcast_fusion
  (45 shorter events, 12.0 us)
Async XLA Ops:
  7.2 15.9 %copy-start.2 = (bf16[8,16,32,128]{3,2,1,0:T(8,128)(2,1)S(1)}, bf16[8,16,32,128]{3,2,1,0:T(8,128)(2,1)}, u32[]{:S(2)}) copy-start(bf16[8,16,32,128]{3,2,1,0:T(8,128)(2,1)} %param.2) | copy-start | bytes 3145732
  7.2 132.9 %all-gather.4.cloned.1.call-start = ((), (), s32[]{:S(2)}) async-start(), calls=%async_computation | async-start | bytes 3145728 | tf_op jit(solution)/shard_map/all_gather | solution.py:76
  8.6 9.5 %collective-permute-start.1 = (bf16[4,16,32,128]{3,2,1,0:T(8,128)(2,1)S(1)}, bf16[4,16,32,128]{3,2,1,0:T(8,128)(2,1)S(1)}, u32[]{:S(2)}, u32[]{:S(2)}) collective-permute-start(bf16[4,16,32,128]{3,2,1,0:T(8,128)(2,1)S(1)} %get-tuple-element.104), channel_id=1, source_target_pairs={{1,0},{2,1},{3,2},{4,3},{5,4},{6,5},{7,6},{8,7},{9,8},{10,9},{11,1... | collective-permute-start | bytes 1572872 | tf_op jit(solution)/shard_map/ppermute | solution.py:23
  8.7 14.4 %collective-permute-start = (bf16[4,16,32,128]{3,2,1,0:T(8,128)(2,1)S(1)}, bf16[4,16,32,128]{3,2,1,0:T(8,128)(2,1)S(1)}, u32[]{:S(2)}, u32[]{:S(2)}) collective-permute-start(bf16[4,16,32,128]{3,2,1,0:T(8,128)(2,1)S(1)} %get-tuple-element.103), channel_id=1, source_target_pairs={{0,1},{1,2},{2,3},{3,4},{4,5},{5,6},{6,7},{7,8},{8,9},{9,10},{10,1... | collective-permute-start | bytes 1572872 | tf_op jit(solution)/shard_map/ppermute | solution.py:20
  40.0 1.6 copy-start.5
  51.7 15.0 %collective-permute-start.3 = (bf16[4,16,32,128]{3,2,1,0:T(8,128)(2,1)S(1)}, bf16[4,16,32,128]{3,2,1,0:T(8,128)(2,1)S(1)}, u32[]{:S(2)}, u32[]{:S(2)}) collective-permute-start(bf16[4,16,32,128]{3,2,1,0:T(8,128)(2,1)S(1)} %get-tuple-element.102), channel_id=1, source_target_pairs={{1,0},{2,1},{3,2},{4,3},{5,4},{6,5},{7,6},{8,7},{9,8},{10,9},{11,1... | collective-permute-start | bytes 1572872 | tf_op jit(solution)/shard_map/ppermute | solution.py:23
  54.2 12.6 %collective-permute-start.2 = (bf16[4,16,32,128]{3,2,1,0:T(8,128)(2,1)S(1)}, bf16[4,16,32,128]{3,2,1,0:T(8,128)(2,1)S(1)}, u32[]{:S(2)}, u32[]{:S(2)}) collective-permute-start(bf16[4,16,32,128]{3,2,1,0:T(8,128)(2,1)S(1)} %get-tuple-element.101), channel_id=1, source_target_pairs={{0,1},{1,2},{2,3},{3,4},{4,5},{5,6},{6,7},{7,8},{8,9},{9,10},{10,1... | collective-permute-start | bytes 1572872 | tf_op jit(solution)/shard_map/ppermute | solution.py:20
  95.1 1.9 copy-start
  95.2 14.7 %collective-permute-start.5 = (bf16[4,16,32,128]{3,2,1,0:T(8,128)(2,1)S(1)}, bf16[4,16,32,128]{3,2,1,0:T(8,128)(2,1)S(1)}, u32[]{:S(2)}, u32[]{:S(2)}) collective-permute-start(bf16[4,16,32,128]{3,2,1,0:T(8,128)(2,1)S(1)} %get-tuple-element.100), channel_id=1, source_target_pairs={{1,0},{2,1},{3,2},{4,3},{5,4},{6,5},{7,6},{8,7},{9,8},{10,9},{11,1... | collective-permute-start | bytes 1572872 | tf_op jit(solution)/shard_map/ppermute | solution.py:23
  95.3 14.6 %collective-permute-start.4 = (bf16[4,16,32,128]{3,2,1,0:T(8,128)(2,1)S(1)}, bf16[4,16,32,128]{3,2,1,0:T(8,128)(2,1)S(1)}, u32[]{:S(2)}, u32[]{:S(2)}) collective-permute-start(bf16[4,16,32,128]{3,2,1,0:T(8,128)(2,1)S(1)} %get-tuple-element.99), channel_id=1, source_target_pairs={{0,1},{1,2},{2,3},{3,4},{4,5},{5,6},{6,7},{7,8},{8,9},{9,10},{10,1... | collective-permute-start | bytes 1572872 | tf_op jit(solution)/shard_map/ppermute | solution.py:20
  97.0 96.0 %all-gather.6.cloned.1.call-start = ((), (), s32[]{:S(2)}) async-start(), calls=%async_computation.1 | async-start | bytes 4456448 | tf_op jit(solution)/shard_map/all_gather | solution.py:58
  125.4 2.0 copy-start.1
  140.1 2.3 %copy-start.4 = (bf16[8,16,32,128]{3,2,1,0:T(8,128)(2,1)S(1)}, bf16[8,16,32,128]{3,2,1,0:T(8,128)(2,1)}, u32[]{:S(2)}) copy-start(bf16[8,16,32,128]{3,2,1,0:T(8,128)(2,1)} %fusion.13) | copy-start | bytes 3145732
  140.1 2.5 %copy-start.3 = (bf16[4096,256]{1,0:T(8,128)(2,1)S(1)}, bf16[4096,256]{1,0:T(8,128)(2,1)}, u32[]{:S(2)}) copy-start(bf16[4096,256]{1,0:T(8,128)(2,1)} %all-gather.4.cloned.1.call-done) | copy-start | bytes 6291460
Sparse Core Ops, SparseCore 0:
  97.2 33.2 all-gather.3
  144.0 48.9 all-gather.5
